TPU v7x, 256 devices: a whole 4x4x8 slice. The times are simulated.
256 devices in a mesh: dp: 16 (over x, y_hi, core), seq: 16 (over z, y_lo).
Axes of the slice: x: 4, y: 4 (y_hi: 2, y_lo: 2; y = y_hi * 2 + y_lo), z: 8, core: 2. Of those that a mesh axis runs over, the one named last changes fastest.
Arguments:
- queries: bfloat16 [40960, 768], P(('dp', 'seq')), may hold values from -8 to 8
- keys: bfloat16 [40960, 768], P(('dp', 'seq')), may hold values from -8 to 8
- values: bfloat16 [40960, 768], P(('dp', 'seq')), may hold values from -6 to 6
- frames: bfloat16 [40960, 768], P(('dp', 'seq')), may hold values from -4 to 4
- upstream: bfloat16 [40960, 768], P(('dp', 'seq')), may hold values from -6 to 6
- lengths: int32 [16], P('dp'), may hold values from 640 to 2560, as said below
- conv_kernel: bfloat16 [32, 768], replicated, may hold values from -1 to 1
Outputs:
- out: bfloat16 [40960, 768], P(('dp', 'seq'))
- query_grad: bfloat16 [40960, 768], P(('dp', 'seq'))
- key_grad: bfloat16 [40960, 768], P(('dp', 'seq'))
- value_grad: bfloat16 [40960, 768], P(('dp', 'seq'))
- frame_grad: bfloat16 [40960, 768], P(('dp', 'seq'))
- kernel_grad: float32 [32, 768], replicated
Inputs may be any that keep to these rules, and one draw needn't show every extreme that they name: `lengths`: one utterance has all 2560 frames live and another has 640.
All inputs are finite; a program needn't handle non-finite values.
Results may differ from a plain program's by a relative error of at most 0.0262.
Values may be sent and summed in bfloat16 or wider, within the bound.
No kernel may reach another device: no remote copies, remote signals or barrier semaphores. Data moves between devices by JAX's collectives and lax.ppermute only.
A program may use at most 128 MiB of HBM per device.

v0:
```python
import jax
import jax.numpy as jnp
from jax import lax
from jax.sharding import PartitionSpec as P

HEAD_DIM = 64
KERNEL = 32


def shifted(x, axis, by):
    count = lax.axis_size(axis)
    pairs = [(i, i + by) for i in range(count) if 0 <= i + by < count]
    return lax.ppermute(x, axis, pairs)


def per_device(queries, keys, values, frames, upstream, lengths, conv_kernel):
    row_count = queries.shape[0]
    channels = queries.shape[1]
    head_count = channels // HEAD_DIM
    seq_count = lax.axis_size("seq")
    first_row = lax.axis_index("seq") * row_count
    length = lengths[0]
    score_scale = HEAD_DIM ** (-0.5)
    span = row_count * seq_count
    shards = 1
    while shards * row_count < 512 and seq_count % (2 * shards) == 0:
        shards = shards * 2
    key_block = row_count * shards
    block_count = span // key_block
    key_all, value_all = (
        lax.all_gather(keys, "seq", axis=0, tiled=True),
        lax.all_gather(values, "seq", axis=0, tiled=True),
    )
    key_blocks = key_all.reshape(block_count, key_block, head_count, HEAD_DIM)
    value_blocks = value_all.reshape(block_count, key_block, head_count, HEAD_DIM)
    block_starts = jnp.arange(block_count, dtype=jnp.int32) * key_block
    query_heads = queries.reshape(row_count, head_count, HEAD_DIM)

    def block_scores(key_part, block_start):
        scores = (
            jnp.einsum("thd,khd->htk", query_heads, key_part, preferred_element_type=jnp.float32)
            * score_scale
        )
        key_live = block_start + jnp.arange(key_part.shape[0], dtype=jnp.int32) < length
        return jnp.where(key_live[None, None, :], scores, -jnp.inf)

    def running_total(state_pair, block_items):
        running_top, total_sum = state_pair
        key_part, block_start = block_items
        scores = block_scores(key_part, block_start)
        higher = jnp.maximum(running_top, jnp.max(scores, axis=2))
        total_sum = total_sum * jnp.exp(running_top - higher) + jnp.sum(
            jnp.exp(scores - higher[:, :, None]), axis=2
        )
        return ((higher, total_sum), None)

    start_state = (
        jnp.full((head_count, row_count), -1e30, jnp.float32),
        jnp.zeros((head_count, row_count), jnp.float32),
    )
    (running_top, total_sum), unused = lax.scan(
        running_total, start_state, (key_blocks, block_starts)
    )
    log_total = running_top + jnp.log(total_sum)

    def attend_block(attend_acc, block_items):
        key_part, value_part, block_start = block_items
        prob_bf = jnp.exp(block_scores(key_part, block_start) - log_total[:, :, None]).astype(
            jnp.bfloat16
        )
        return (
            attend_acc
            + jnp.einsum("htk,khd->thd", prob_bf, value_part, preferred_element_type=jnp.float32),
            None,
        )

    attend_acc, unused = lax.scan(
        attend_block,
        jnp.zeros((row_count, head_count, HEAD_DIM), jnp.float32),
        (key_blocks, value_blocks, block_starts),
    )
    attended = attend_acc.reshape(row_count, channels).astype(jnp.bfloat16)
    frame_live = (first_row + jnp.arange(row_count, dtype=jnp.int32) < length)[:, None]
    hidden = (frames.astype(jnp.float32) + attended.astype(jnp.float32)).astype(jnp.bfloat16)
    masked = jnp.where(frame_live, hidden, jnp.zeros_like(hidden))
    past_rows = shifted(masked[row_count - (KERNEL - 1) :], "seq", 1)
    extended = jnp.concatenate([past_rows, masked], axis=0).astype(jnp.float32)
    weights = conv_kernel.astype(jnp.float32)
    conv_out = jnp.zeros((row_count, channels), jnp.float32)
    for tap_index in range(KERNEL):
        conv_out = (
            conv_out
            + weights[tap_index]
            * extended[KERNEL - 1 - tap_index : KERNEL - 1 - tap_index + row_count]
        )
    sig_conv = jax.nn.sigmoid(conv_out)
    out = (hidden.astype(jnp.float32) + conv_out * sig_conv).astype(jnp.bfloat16)
    loss_grad = jnp.where(frame_live, upstream.astype(jnp.float32), 0.0)
    conv_grad = (loss_grad * sig_conv * (1.0 + conv_out * (1.0 - sig_conv))).astype(jnp.bfloat16)
    conv_float = conv_grad.astype(jnp.float32)
    kernel_part = jnp.stack(
        [
            jnp.sum(
                conv_float * extended[KERNEL - 1 - tap_index : KERNEL - 1 - tap_index + row_count],
                axis=0,
            )
            for tap_index in range(KERNEL)
        ]
    )
    future_rows = shifted(conv_grad[: KERNEL - 1], "seq", -1)
    ahead_rows = jnp.concatenate([conv_grad, future_rows], axis=0).astype(jnp.float32)
    back_conv = jnp.zeros((row_count, channels), jnp.float32)
    for tap_index in range(KERNEL):
        back_conv = back_conv + weights[tap_index] * ahead_rows[tap_index : tap_index + row_count]
    frame_grad = (loss_grad + jnp.where(frame_live, back_conv, 0.0)).astype(jnp.bfloat16)
    grad_heads = frame_grad.reshape(row_count, head_count, HEAD_DIM)
    attended_heads = attended.reshape(row_count, head_count, HEAD_DIM)
    delta_rows = jnp.sum(
        grad_heads.astype(jnp.float32) * attended_heads.astype(jnp.float32), axis=2
    ).T

    def score_grads(key_part, value_part, block_start):
        soft_weights = jnp.exp(block_scores(key_part, block_start) - log_total[:, :, None])
        prob_grad = jnp.einsum(
            "thd,khd->htk", grad_heads, value_part, preferred_element_type=jnp.float32
        )
        score_grad = (soft_weights * (prob_grad - delta_rows[:, :, None])).astype(jnp.bfloat16)
        return (soft_weights.astype(jnp.bfloat16), score_grad)

    def gradient_block(query_acc, block_items):
        key_part, value_part, block_start = block_items
        prob_bf, score_grad = score_grads(key_part, value_part, block_start)
        query_acc = query_acc + jnp.einsum(
            "htk,khd->thd", score_grad, key_part, preferred_element_type=jnp.float32
        )
        key_term = (
            jnp.einsum("htk,thd->khd", score_grad, query_heads, preferred_element_type=jnp.float32)
            * score_scale
        )
        value_term = jnp.einsum(
            "htk,thd->khd", prob_bf, grad_heads, preferred_element_type=jnp.float32
        )
        grad_terms = jnp.concatenate(
            [key_term.reshape(key_block, channels), value_term.reshape(key_block, channels)], axis=1
        )
        return (query_acc, grad_terms)

    query_acc, grad_terms = lax.scan(
        gradient_block,
        jnp.zeros((row_count, head_count, HEAD_DIM), jnp.float32),
        (key_blocks, value_blocks, block_starts),
    )
    own_rows = lax.psum_scatter(
        grad_terms.reshape(span, 2 * channels).astype(jnp.bfloat16),
        "seq",
        scatter_dimension=0,
        tiled=True,
    ).astype(jnp.float32)
    key_grad = own_rows[:, :channels].astype(jnp.bfloat16)
    value_grad = own_rows[:, channels:].astype(jnp.bfloat16)
    query_grad = (query_acc * score_scale).reshape(row_count, channels).astype(jnp.bfloat16)
    kernel_total = lax.psum(kernel_part, ("dp", "seq"))
    kernel_grad = kernel_total / lax.axis_size("dp")
    return (out, query_grad, key_grad, value_grad, frame_grad, kernel_grad)


def solution(mesh):
    placed = (
        P(("dp", "seq"), None),
        P(("dp", "seq"), None),
        P(("dp", "seq"), None),
        P(("dp", "seq"), None),
        P(("dp", "seq"), None),
        P("dp"),
        P(),
    )
    return jax.shard_map(
        per_device,
        mesh=mesh,
        in_specs=placed,
        out_specs=(
            P(("dp", "seq"), None),
            P(("dp", "seq"), None),
            P(("dp", "seq"), None),
            P(("dp", "seq"), None),
            P(("dp", "seq"), None),
            P(),
        ),
        check_vma=False,
    )
```

profile of v0, /device:TPU:1, one launch (start us, length us, event | category | flops | bytes accessed | tf_op | source)
XLA Modules:
  0.0 772.7 jit_solution(14482289051030039429)
XLA Ops:
  13.8 92.2 %all-gather.5.cloned.1.call-done = bf16[2560,768]{1,0:T(8,128)(2,1)} async-done(((bf16[160,768]{1,0:T(8,128)(2,1)}), bf16[2560,768]{1,0:T(8,128)(2,1)}) %all-gather.5.cloned.1.call-update) | async-done | bytes 3932176 | tf_op jit(solution)/shard_map/all_gather | solution.py:31
  106.1 6.2 copy.23
  112.3 7.6 reshape.64
  119.9 82.5 %all-gather.3.cloned.1.call-done = bf16[2560,768]{1,0:T(8,128)(2,1)} async-done(((bf16[160,768]{1,0:T(8,128)(2,1)}), bf16[2560,768]{1,0:T(8,128)(2,1)}) %all-gather.3.cloned.1.call-update) | async-done | bytes 3932176 | tf_op jit(solution)/shard_map/all_gather | solution.py:32
  202.4 6.2 copy.22
  208.6 7.6 reshape.63
  216.2 5.0 copy.26
  221.2 2.7 copy.25
  223.9 22.7 %while.37 = (s32[]{:T(128)}, f32[12,160]{1,0:T(8,128)S(1)}, f32[12,160]{1,0:T(8,128)S(1)}, s32[4]{0:T(128)S(1)}, s32[]{:T(128)}, /*index=5*/bf16[4,640,12,64]{1,...) while((s32[]{:T(128)}, f32[12,160]{1,0:T(8,128)S(1)}, ...), condition=%wide.region_3.4_spmd.clone, body=%wide.region_0.3_spmd.clone.sunk | while | flops 165898880 | bytes 11161096 | solution.py:61
  246.6 43.0 %while.38 = (s32[]{:T(128)}, f32[160,12,64]{0,2,1:T(8,128)}, bf16[4,640,12,64]{1,3,2,0:T(8,128)(2,1)}, s32[4]{0:T(128)S(1)}, s32[]{:T(128)}, /*index=5*/bf16[4,6...) while((s32[]{:T(128)}, f32[160,12,64]{0,2,1:T(8,128)}, ...), condition=%wide.region_5.6_spmd.clone, body=%wide.region_4.5_spmd.clone.sunk | while | flops 319735040 | bytes 5464979 | solution.py:77
  248.5 4.5 constant_dynamic-slice_fusion.2
  253.0 4.2 fusion.150
  259.1 4.5 constant_dynamic-slice_fusion.2
  263.6 4.4 fusion.150
  269.9 4.5 constant_dynamic-slice_fusion.2
  274.4 4.4 fusion.150
  280.7 4.5 constant_dynamic-slice_fusion.2
  285.2 4.4 fusion.150
  291.1 2.7 collective-permute-start
  297.1 14.6 %fusion.79 = (f32[768]{0:T(1024)S(1)}, f32[768]{0:T(1024)S(1)}, f32[768]{0:T(1024)S(1)}, f32[768]{0:T(1024)S(1)}, f32[768]{0:T(1024)S(1)}, /*index=5*/f32[768]{0...) fusion(f32[191,768]{0,1:T(8,128)S(1)} %maximum_convert_fusion, ...), kind=kLoop, calls=%fused_computation.121 | loop fusion | flops 13625856 | bytes 16865440 | tf_op jit(solution)/shard_map/reduce_sum | solution.py:103
  312.9 4.7 fusion.78
  336.5 5.4 stack.131
  342.4 13.5 %fusion.83 = bf16[160,768]{0,1:T(8,128)(2,1)S(1)} fusion(f32[191,768]{0,1:T(8,128)S(1)} %maximum_convert_fusion.1, bf16[160,768]{0,1:T(8,128)(2,1)S(1)} %copy.29, f32[768]{0:T(1024)S(1)} %get-tuple-element.320, f32[768]{0:T(1024)S(1)} %get-tuple-element.321, f32[768]{0:T(1024)S(1)} %get-tuple-element.322, f32[768]{0:T(1024)} %get-tuple-element.323, ...), kind=kLoop, calls=%fused_computation.126 | loop fusion | flops 8355840 | bytes 16318624 | tf_op jit(solution)/shard_map/convert_element_type | solution.py:115
  356.1 50.8 %while.39 = (s32[]{:T(128)}, f32[160,12,64]{0,2,1:T(8,128)S(1)}, bf16[4,640,1536]{1,2,0:T(8,128)(2,1)}, bf16[4,640,12,64]{1,3,2,0:T(8,128)(2,1)}, s32[4]{0:T(128...) while((s32[]{:T(128)}, f32[160,12,64]{0,2,1:T(8,128)S(1)}, ...), condition=%wide.region_8.9_spmd.clone, body=%wide.region_7.8_spmd.clone.sunk | while | flops 803882240 | bytes 32956980 | solution.py:148
  361.4 3.0 multiply_convert_fusion.5
  374.1 3.0 multiply_convert_fusion.5
  386.8 3.0 multiply_convert_fusion.5
  399.5 3.0 multiply_convert_fusion.5
  402.5 2.4 fusion.162
  406.9 10.7 %copy.32 = bf16[4,640,1536]{2,1,0:T(8,128)(2,1)} copy(bf16[4,640,1536]{1,2,0:T(8,128)(2,1)} %get-tuple-element.148) | data formatting | bytes 15728640 | tf_op jit(solution)/shard_map/convert_element_type | solution.py:154
  421.6 172.5 %all-reduce.2.cloned.1.call-done = f32[32,768]{1,0:T(8,128)} async-done(((f32[32,768]{1,0:T(8,128)}), f32[32,768]{1,0:T(8,128)}) %all-reduce.2.cloned.1.call-update) | async-done | bytes 98320 | tf_op jit(solution)/shard_map/psum | solution.py:162
  595.6 168.7 %reduce-scatter.2.cloned.1.call-done = bf16[160,1536]{1,0:T(8,128)(2,1)} async-done(((bf16[2560,1536]{1,0:T(8,128)(2,1)}), bf16[160,1536]{1,0:T(8,128)(2,1)}) %reduce-scatter.2.cloned.1.call-update) | async-done | bytes 491536 | tf_op jit(solution)/shard_map/reduce_scatter | solution.py:153
  (153 shorter events, 105.0 us)
Async XLA Ops:
  7.2 98.9 %all-gather.5.cloned.1.call-start = ((), (), s32[]{:S(2)}) async-start(), calls=%async_computation.2 | async-start | bytes 4177920 | tf_op jit(solution)/shard_map/all_gather | solution.py:31
  7.9 194.5 %all-gather.3.cloned.1.call-start = ((), (), s32[]{:S(2)}) async-start(), calls=%async_computation.1 | async-start | bytes 4177920 | tf_op jit(solution)/shard_map/all_gather | solution.py:32
  8.6 585.4 %all-reduce.2.cloned.1.call-start = ((), (), s32[]{:S(2)}) async-start(), calls=%async_computation.4 | async-start | bytes 196608 | tf_op jit(solution)/shard_map/psum | solution.py:162
  10.2 102.1 %copy-start.3 = (f32[32,768]{1,0:T(8,128)}, f32[32,768]{1,0:T(8,128)S(1)}, u32[]{:S(2)}) copy-start(f32[32,768]{1,0:T(8,128)S(1)} %convert_element_type.78) | copy-start | bytes 294916
  13.1 277.8 %copy-start.6 = (pred[160]{0:T(512)(128)(4,1)}, pred[160]{0:T(512)(128)(4,1)S(1)}, u32[]{:S(2)}) copy-start(pred[160]{0:T(512)(128)(4,1)S(1)} %add_compare_fusion.3) | copy-start | bytes 484
  216.2 5.0 copy-start
  289.6 6.1 copy-start.4
  289.6 6.1 copy-start.7
  291.1 5.8 collective-permute-start
  311.6 30.6 %collective-permute-start.1 = (bf16[31,768]{0,1:T(8,128)(2,1)S(1)}, bf16[31,768]{0,1:T(8,128)(2,1)S(1)}, u32[]{:S(2)}, u32[]{:S(2)}) collective-permute-start(bf16[31,768]{0,1:T(8,128)(2,1)S(1)} %slice.531), channel_id=1, source_target_pairs={{1,0},{2,1},{3,2},{4,3},{5,4},{6,5},{7,6},{8,7},{9,8},{10,9},{11,1... | collective-permute-start | bytes 142856 | tf_op jit(solution)/shard_map/ppermute | solution.py:13
  342.0 422.3 %reduce-scatter.2.cloned.1.call-start = ((), (), s32[]{:S(2)}) async-start(), calls=%async_computation.3 | async-start | bytes 8355840 | tf_op jit(solution)/shard_map/reduce_scatter | solution.py:153
  342.4 13.5 %copy-start.2 = (f32[160,12,64]{0,2,1:T(8,128)S(1)}, f32[160,12,64]{0,2,1:T(8,128)}, u32[]{:S(2)}) copy-start(f32[160,12,64]{0,2,1:T(8,128)} %get-tuple-element.146) | copy-start | bytes 1474564
  342.4 13.7 %copy-start.5 = (f32[12,160]{1,0:T(8,128)S(1)}, f32[12,160]{1,0:T(8,128)}, u32[]{:S(2)}) copy-start(f32[12,160]{1,0:T(8,128)} %copy-done.4) | copy-start | bytes 23044
  342.4 13.7 %copy-start.8 = (s32[4]{0:T(128)S(1)}, s32[4]{0:T(128)}, u32[]{:S(2)}) copy-start(s32[4]{0:T(128)} %copy-done.7) | copy-start | bytes 52
  417.6 1.1 copy-start.1
Sparse Core Ops, SparseCore 0:
  9.8 96.2 all-gather.4
  107.8 94.5 all-gather.2
  342.1 251.9 all-reduce.1
  596.5 167.7 reduce-scatter.1
where the time goes:
time: 775 us; the launch traced here: 773 us
  waiting for transfers between devices  517 us (67%)
  local copies, waits for them, and re-layouts  108 us (14%)
  other arithmetic  64.8 us (8%)
  matrix products  63.5 us (8%)
  between operations  14.7 us (2%)
    psum x1, waiting for transfers between devices, per_device(): kernel_total = lax.psum(kernel_part, ('dp', 'seq'))  173 us
    reduce_scatter x1, waiting for transfers between devices, per_device(): lax.psum_scatter(grad_terms.reshape(span, 2 * channels).astype(jnp.bfloat...  169 us
    all_gather x1, waiting for transfers between devices, per_device(): lax.all_gather(keys, 'seq', axis=0, tiled=True)  92.2 us
    all_gather x1, waiting for transfers between devices, per_device(): lax.all_gather(values, 'seq', axis=0, tiled=True)  82.5 us
    dynamic_slice x16, local copies, waits for them, and re-layouts, per_device(): lax.scan(running_total, start_state, (key_blocks, block_starts))  24.9 us
    another operation x33, local copies, waits for them, and re-layouts, per_device(): jnp.stack([jnp.sum(conv_float * extended[KERNEL - 1 - tap_index:KERNEL -...  24.3 us
    reduce_sum x2, other arithmetic, per_device(): jnp.sum(conv_float * extended[KERNEL - 1 - tap_index:KERNEL - 1 - tap_ind...  19.2 us
    dot_general x4, matrix products, attend_block(): jnp.einsum('htk,khd->thd', prob_bf, value_part, preferred_element_type=jn...  17.5 us
  transfers between devices with their start and end apart: 6, of which 4 were waited for; matrix products, arithmetic and copies ran while one was open for 17% of the time, Pallas kernels for 0%

commit v1 on v0

--- a/solution.py
+++ b/solution.py
@@ -159,7 +159,7 @@
     key_grad = own_rows[:, :channels].astype(jnp.bfloat16)
     value_grad = own_rows[:, channels:].astype(jnp.bfloat16)
     query_grad = (query_acc * score_scale).reshape(row_count, channels).astype(jnp.bfloat16)
-    kernel_total = lax.psum(kernel_part, ("dp", "seq"))
+    kernel_total = jnp.sum(lax.all_gather(kernel_part, ("dp", "seq")), axis=0)
     kernel_grad = kernel_total / lax.axis_size("dp")
     return (out, query_grad, key_grad, value_grad, frame_grad, kernel_grad)
 

time: 775 us -> 1350 us (1.74)
  waiting for transfers between devices: 517 us -> 1090 us
  local copies, waits for them, and re-layouts: 108 us -> 68.3 us
  matrix products: 63.5 us -> 83.4 us
    all_gather x0 -> x1, waiting for transfers between devices: none -> 744 us  [per_device(): kernel_total = jnp.sum(lax.all_gather(kernel_part, ('dp', 'seq')), axis=0)]
    psum x1 -> x0, waiting for transfers between devices: 173 us -> none  [per_device(): kernel_total = lax.psum(kernel_part, ('dp', 'seq'))]
    another operation x33, local copies, waits for them, and re-layouts: 24.3 us -> 2.73 us  [per_device(): jnp.stack([jnp.sum(conv_float * extended[KERNEL - 1 - tap_index:KERNEL -...]
    dynamic_slice x16 -> x12, local copies, waits for them, and re-layouts: 24.9 us -> 7.37 us  [per_device(): lax.scan(running_total, start_state, (key_blocks, block_starts))]
    all_gather x1, waiting for transfers between devices: 92.2 us -> 77.7 us  [per_device(): lax.all_gather(keys, 'seq', axis=0, tiled=True)]
  transfers between devices with their start and end apart: 6 -> 6, of which waited for: 4 -> 6; matrix products, arithmetic and copies ran while one was open for 17% -> 3% of each run, Pallas kernels for 0% -> 0%
where the time goes in v1:
time: 1350 us; the launch traced here: 1340 us
  waiting for transfers between devices  1090 us (81%)
  matrix products  83.4 us (6%)
  other arithmetic  77.9 us (6%)
  local copies, waits for them, and re-layouts  68.3 us (5%)
  between operations  15.1 us (1%)
    all_gather x1, waiting for transfers between devices, per_device(): kernel_total = jnp.sum(lax.all_gather(kernel_part, ('dp', 'seq')), axis=0)  744 us
    reduce_scatter x1, waiting for transfers between devices, per_device(): lax.psum_scatter(grad_terms.reshape(span, 2 * channels).astype(jnp.bfloat...  166 us
    all_gather x1, waiting for transfers between devices, per_device(): lax.all_gather(values, 'seq', axis=0, tiled=True)  92.6 us
    all_gather x1, waiting for transfers between devices, per_device(): lax.all_gather(keys, 'seq', axis=0, tiled=True)  77.7 us
  transfers between devices with their start and end apart: 6, of which 6 were waited for; matrix products, arithmetic and copies ran while one was open for 3% of the time, Pallas kernels for 0%

profile of v1, /device:TPU:1, one launch (start us, length us, event | category | flops | bytes accessed | tf_op | source)
XLA Modules:
  0.0 1339.5 jit_solution(7572825218616453015)
XLA Ops:
  13.4 92.6 %all-gather.5.cloned.1.call-done = bf16[2560,768]{1,0:T(8,128)(2,1)} async-done(((bf16[160,768]{1,0:T(8,128)(2,1)}), bf16[2560,768]{1,0:T(8,128)(2,1)}) %all-gather.5.cloned.1.call-update) | async-done | bytes 3932176 | tf_op jit(solution)/shard_map/all_gather | solution.py:32
  106.1 6.2 copy.37
  112.3 7.6 reshape.63
  119.9 4.8 copy.41
  124.7 77.7 %all-gather.7.cloned.1.call-done = bf16[2560,768]{1,0:T(8,128)(2,1)} async-done(((bf16[160,768]{1,0:T(8,128)(2,1)}), bf16[2560,768]{1,0:T(8,128)(2,1)}) %all-gather.7.cloned.1.call-update) | async-done | bytes 3932176 | tf_op jit(solution)/shard_map/all_gather | solution.py:31
  202.4 6.2 copy.38
  208.7 7.6 reshape.64
  216.3 4.7 copy.42
  221.0 39.7 %while.37 = (s32[]{:T(128)}, f32[12,160]{1,0:T(8,128)S(1)}, f32[12,160]{1,0:T(8,128)S(1)}, s32[4]{0:T(128)S(1)}, s32[]{:T(128)}, /*index=5*/bf16[4,640,12,64]{1,...) while((s32[]{:T(128)}, f32[12,160]{1,0:T(8,128)S(1)}, f32[12,160]{1,0:T(8,128)S(1)}, ...), condition=%wide.region_3.4_spmd.clone, body=%wide.region_0.3_spmd.clone.sunk | while | flops 165898880 | bytes 11308552 | solution.py:61
  222.9 4.4 bitcast_reduce_fusion.2
  227.3 3.6 fusion.145
  232.8 4.3 bitcast_reduce_fusion.2
  237.2 3.6 fusion.145
  242.8 4.4 bitcast_reduce_fusion.2
  247.1 3.6 fusion.145
  252.7 4.4 bitcast_reduce_fusion.2
  257.1 3.6 fusion.145
  260.8 23.3 %while.38 = (s32[]{:T(128)}, f32[160,12,64]{0,2,1:T(8,128)S(1)}, bf16[4,640,12,64]{1,3,2,0:T(8,128)(2,1)}, s32[4]{0:T(128)S(1)}, s32[]{:T(128)}, /*index=5*/bf16...) while((s32[]{:T(128)}, f32[160,12,64]{0,2,1:T(8,128)S(1)}, ...), condition=%wide.region_5.6_spmd.clone, body=%wide.region_4.5_spmd.clone.sunk | while | flops 319735040 | bytes 3352970 | solution.py:77
  262.7 3.9 fusion.150
  268.5 3.9 fusion.150
  274.3 3.9 fusion.150
  280.2 3.9 fusion.150
  290.7 13.6 %fusion.78 = (f32[768]{0:T(1024)S(1)}, f32[768]{0:T(1024)}, f32[768]{0:T(1024)}, f32[768]{0:T(1024)}, f32[768]{0:T(1024)}, /*index=5*/f32[768]{0:T(1024)}, f32[7...) fusion(f32[191,768]{0,1:T(8,128)S(1)} %maximum_convert_fusion, ...), kind=kLoop, calls=%fused_computation.119 | loop fusion | flops 13625856 | bytes 16865440 | tf_op jit(solution)/shard_map/reduce_sum | solution.py:103
  305.8 6.3 collective-permute-done.1
  312.2 10.8 fusion.82
  323.8 64.2 %while.39 = (s32[]{:T(128)}, f32[160,12,64]{0,2,1:T(8,128)}, bf16[4,640,1536]{1,2,0:T(8,128)(2,1)}, bf16[4,640,12,64]{1,3,2,0:T(8,128)(2,1)}, s32[4]{0:T(128)S(1...) while((s32[]{:T(128)}, f32[160,12,64]{0,2,1:T(8,128)}, ...), condition=%wide.region_8.9_spmd.clone, body=%wide.region_7.8_spmd.clone.sunk | while | flops 803882240 | bytes 73704064 | solution.py:148
  362.9 3.6 fusion.162
  387.9 10.7 copy.46
  399.7 4.7 fusion.77
  411.6 165.7 %reduce-scatter.2.cloned.1.call-done = bf16[160,1536]{1,0:T(8,128)(2,1)} async-done(((bf16[2560,1536]{1,0:T(8,128)(2,1)}), bf16[160,1536]{1,0:T(8,128)(2,1)}) %reduce-scatter.2.cloned.1.call-update) | async-done | bytes 491536 | tf_op jit(solution)/shard_map/reduce_scatter | solution.py:153
  579.1 743.8 %all-gather.9.cloned.1.call-done = f32[8192,768]{1,0:T(8,128)} async-done(((f32[32,768]{1,0:T(8,128)}), f32[8192,768]{1,0:T(8,128)}) %all-gather.9.cloned.1.call-update) | async-done | bytes 25165840 | tf_op jit(solution)/shard_map/all_gather | solution.py:162
  1322.9 9.4 reduce_sum.348
  (203 shorter events, 100.1 us)
Async XLA Ops:
  7.2 98.9 %all-gather.5.cloned.1.call-start = ((), (), s32[]{:S(2)}) async-start(), calls=%async_computation.1 | async-start | bytes 4177920 | tf_op jit(solution)/shard_map/all_gather | solution.py:32
  7.9 194.5 %all-gather.7.cloned.1.call-start = ((), (), s32[]{:S(2)}) async-start(), calls=%async_computation.2 | async-start | bytes 4177920 | tf_op jit(solution)/shard_map/all_gather | solution.py:31
  8.6 568.6 %reduce-scatter.2.cloned.1.call-start = ((), (), s32[]{:S(2)}) async-start(), calls=%async_computation.3 | async-start | bytes 8355840 | tf_op jit(solution)/shard_map/reduce_scatter | solution.py:153
  12.4 271.8 %copy-start.7 = (bf16[160,768]{0,1:T(8,128)(2,1)}, bf16[160,768]{0,1:T(8,128)(2,1)S(1)}, u32[]{:S(2)}) copy-start(bf16[160,768]{0,1:T(8,128)(2,1)S(1)} %copy.36) | copy-start | bytes 737284
  260.8 27.3 %copy-start.12 = (bf16[160,768]{1,0:T(8,128)(2,1)S(1)}, bf16[160,768]{1,0:T(8,128)(2,1)}, u32[]{:S(2)}) copy-start(bf16[160,768]{1,0:T(8,128)(2,1)} %param.17) | copy-start | bytes 737284
  285.3 5.2 collective-permute-start
  304.2 18.8 %copy-start.5 = (bf16[160,768]{0,1:T(8,128)(2,1)}, bf16[160,768]{0,1:T(8,128)(2,1)S(1)}, u32[]{:S(2)}) copy-start(bf16[160,768]{0,1:T(8,128)(2,1)S(1)} %get-tuple-element.435) | copy-start | bytes 737284
  304.3 7.8 collective-permute-start.1
  325.9 4.9 copy-start
  341.8 4.9 copy-start
  357.9 4.9 copy-start
  371.8 4.1 copy-start.10
  374.0 4.9 copy-start
  398.6 8.9 copy-start.4
  398.6 8.9 copy-start.8
  398.7 11.1 copy-start.11
  398.7 12.0 copy-start.2
  398.7 924.2 %all-gather.9.cloned.1.call-start = ((), (), s32[]{:S(2)}) async-start(), calls=%async_computation.4 | async-start | bytes 25264128 | tf_op jit(solution)/shard_map/all_gather | solution.py:162
  399.6 4.8 copy-start.26
  399.6 4.9 copy-start.25
  399.6 4.9 copy-start.24
  399.6 4.9 copy-start.23
  399.6 4.9 copy-start.22
  399.6 4.9 copy-start.21
  399.6 4.9 copy-start.20
  399.6 4.9 copy-start.19
  399.7 5.0 copy-start.18
  399.7 5.0 copy-start.17
  399.7 5.0 copy-start.16
  399.7 5.0 copy-start.15
  399.7 5.0 copy-start.14
  399.7 5.0 copy-start.13
  (10 other events, 29.1 us)
Sparse Core Ops, SparseCore 0:
  9.8 96.2 all-gather.4
  107.8 94.5 all-gather.6
  398.8 178.4 reduce-scatter.1
  579.5 743.2 all-gather.8
